TPU v7x, 32 devices: a whole 2x2x4 slice. The times are simulated.
32 devices in a mesh: grp: 2 (over y), row: 4 (over z), head: 2 (over x), rep: 2 (over core).
Axes of the slice: x: 2, y: 2, z: 4, core: 2. Of those that a mesh axis runs over, the one named last changes fastest.
Arguments:
- queries: float32 [2048, 8192], P(('grp', 'row', 'rep'), 'head'), parts along dimension 0
- key_max: float32 [4096, 1024], P(('grp', 'row', 'rep'), 'head'), parts along dimension 0
- key_min: float32 [4096, 1024], P(('grp', 'row', 'rep'), 'head'), parts along dimension 0, as said below
- limits: int32 [2048], P(('grp', 'row', 'rep')), parts along dimension 0, may hold values from 0 to 2047, as said below
Outputs:
- page_mass: float32 [2048, 2048], P(('grp', 'row', 'rep'), 'head'), parts along dimension 0
There are 2 independent parts, one for each index of `grp`. A program takes and returns all parts, laid end to end along the dimension named above; each array names one. Nothing has to cross between parts.
Inputs may be any that keep to these rules, and one draw needn't show every extreme that they name: key_min <= key_max in every entry. Rows of the i-th aligned block of 128 rows have limits within the i-th block of 256 pages, not falling within a block; the first block's first row has the first page and the last block's last row the last page.
All inputs are finite; a program needn't handle non-finite values.
Results may differ from a plain program's by a relative error of at most 0.00013.
Values sent between devices are 32-bit elements; how exact they have to be, the bound alone decides.
No kernel may reach another device: no remote copies, remote signals or barrier semaphores. Data moves between devices by JAX's collectives and lax.ppermute only.
A program may use at most 64 MiB of HBM per device.

v0:
```python
import math
import jax
import jax.numpy as jnp
from jax import lax
from jax.sharding import PartitionSpec as P

DH = 128


def per_device(queries, key_max, key_min, limits):
    head_count = queries.shape[1] // DH
    kv_count = key_max.shape[1] // DH
    group_size = head_count // kv_count
    score_scale = 1.0 / math.sqrt(DH)
    bounds = jnp.stack((key_max, key_min))
    query_rows, row_limits = (queries, limits)
    gathered = lax.all_gather(bounds, ("row", "rep"), axis=1, tiled=True)
    page_ids = jnp.arange(gathered.shape[1], dtype=jnp.int32)
    row_count = query_rows.shape[0]
    page_count = gathered.shape[1]
    head_rows = query_rows.reshape(row_count, head_count, DH).transpose(1, 0, 2)
    positive = jnp.maximum(head_rows, 0.0)
    negative = jnp.minimum(head_rows, 0.0)
    sheets = gathered.reshape(2, page_count, kv_count, DH).transpose(2, 0, 1, 3)
    visible = page_ids[None, :] <= row_limits[:, None]

    def head_scores(head_index, kv_index):
        upper_part = jnp.dot(
            positive[head_index], sheets[kv_index, 0].T, precision=lax.Precision.HIGHEST
        )
        return upper_part + jnp.dot(
            negative[head_index], sheets[kv_index, 1].T, precision=lax.Precision.HIGHEST
        )

    def head_step(accumulated, head_index):
        raw_scores = head_scores(head_index, head_index // group_size)
        masked = jnp.where(visible, raw_scores * score_scale, -1e30)
        row_top = jnp.max(masked, axis=1, keepdims=True)
        weights = jnp.exp(masked - row_top)
        row_total = jnp.sum(weights, axis=1, keepdims=True)
        return (accumulated + weights / row_total, None)

    start = jnp.zeros((row_count, page_count), jnp.float32)
    accumulated, unused = lax.scan(head_step, start, jnp.arange(head_count, dtype=jnp.int32))
    return lax.psum_scatter(accumulated, "head", scatter_dimension=1, tiled=True)


def solution(mesh):
    placed = (
        P(("grp", "row", "rep"), "head"),
        P(("grp", "row", "rep"), "head"),
        P(("grp", "row", "rep"), "head"),
        P(("grp", "row", "rep")),
    )
    return jax.shard_map(
        per_device,
        mesh=mesh,
        in_specs=placed,
        out_specs=P(("grp", "row", "rep"), "head"),
        check_vma=False,
    )
```

profile of v0, /device:TPU:0, one launch (start us, length us, event | category | flops | bytes accessed | tf_op | source)
XLA Modules:
  0.0 448.6 jit_solution(9973003947528456110)
XLA Ops:
  14.3 80.7 %all-gather.2.cloned.1.call-done = f32[2,2048,512]{1,2,0:T(8,128)} async-done(((f32[2,256,512]{1,2,0:T(8,128)}), f32[2,2048,512]{1,2,0:T(8,128)}) %all-gather.2.cloned.1.call-update) | async-done | bytes 8388624 | tf_op jit(solution)/shard_map/all_gather | solution.py:17
  95.0 8.7 %copy.10 = f32[4,2,2048,128]{3,2,1,0:T(8,128)} copy(f32[4,2,2048,128]{2,3,0,1:T(8,128)} %bitcast.40) | data formatting | bytes 16777216
  103.8 318.0 %while.13 = (s32[]{:T(128)}, f32[128,2048]{1,0:T(8,128)S(1)}, s32[32]{0:T(128)S(1)}, f32[32,128,128]{1,2,0:T(8,128)}, f32[4,2,2048,128]{3,2,1,0:T(8,128)}, /*ind...) while((s32[]{:T(128)}, f32[128,2048]{1,0:T(8,128)S(1)}, ...), condition=%wide.region_3.4_spmd.clone, body=%wide.region_0.3_spmd.clone.sunk | while | flops 808189696 | bytes 9571716 | solution.py:44
  110.4 2.6 fusion.26
  120.4 2.6 fusion.26
  140.3 2.6 fusion.26
  160.1 2.6 fusion.26
  170.1 2.6 fusion.26
  180.0 2.6 fusion.26
  189.9 2.6 fusion.26
  199.9 2.6 fusion.26
  209.8 2.6 fusion.26
  219.7 2.6 fusion.26
  239.6 2.6 fusion.26
  249.6 2.6 fusion.26
  259.5 2.6 fusion.26
  269.4 2.6 fusion.26
  279.4 2.6 fusion.26
  289.3 2.6 fusion.26
  299.2 2.6 fusion.26
  309.2 2.6 fusion.26
  319.1 2.6 fusion.26
  339.0 2.6 fusion.26
  348.9 2.6 fusion.26
  358.9 2.6 fusion.26
  368.8 2.6 fusion.26
  378.7 2.6 fusion.26
  388.7 2.6 fusion.26
  398.6 2.6 fusion.26
  408.5 2.6 fusion.26
  418.5 2.6 fusion.26
  422.7 19.0 %reduce-scatter.2.cloned.1.call-done = f32[128,1024]{1,0:T(8,128)} async-done(((f32[128,2048]{1,0:T(8,128)}), f32[128,1024]{1,0:T(8,128)}) %reduce-scatter.2.cloned.1.call-update) | async-done | bytes 524304 | tf_op jit(solution)/shard_map/reduce_scatter | solution.py:45
  (147 shorter events, 133.7 us)
Async XLA Ops:
  6.5 88.5 %all-gather.2.cloned.1.call-start = ((), (), s32[]{:S(2)}) async-start(), calls=%async_computation.1 | async-start | bytes 9437184 | tf_op jit(solution)/shard_map/all_gather | solution.py:17
  10.1 431.6 %reduce-scatter.2.cloned.1.call-start = ((), (), s32[]{:S(2)}) async-start(), calls=%async_computation.2 | async-start | bytes 1572864 | tf_op jit(solution)/shard_map/reduce_scatter | solution.py:45
  95.0 8.8 %copy-start.1 = (s32[128]{0:T(128)S(1)}, s32[128]{0:T(128)}, u32[]{:S(2)}) copy-start(s32[128]{0:T(128)} %param.9) | copy-start | bytes 1540
  421.7 1.0 copy-start
Sparse Core Ops, SparseCore 0:
  10.2 84.7 all-gather.1
  422.9 18.8 reduce-scatter.1
where the time goes:
time: 452 us; the launch traced here: 449 us
  matrix products  157 us (35%)
  loops' own time  121 us (27%)
  waiting for transfers between devices  99.8 us (22%)
  local copies, waits for them, and re-layouts  33.2 us (7%)
  other arithmetic  24.4 us (5%)
  between operations  13.4 us (3%)
    another operation x1, loops' own time, per_device(): lax.scan(head_step, start, jnp.arange(head_count, dtype=jnp.int32))  121 us
    dot_general x32, matrix products, head_scores(): jnp.dot(negative[head_index], sheets[kv_index, 1].T, precision=lax.Precis...  82.2 us
    all_gather x1, waiting for transfers between devices, per_device(): gathered = lax.all_gather(bounds, ('row', 'rep'), axis=1, tiled=True)  80.7 us
    dot_general x32, matrix products, head_scores(): jnp.dot(positive[head_index], sheets[kv_index, 0].T, precision=lax.Precis...  74.5 us
    dynamic_slice x32, local copies, waits for them, and re-layouts, per_device(): lax.scan(head_step, start, jnp.arange(head_count, dtype=jnp.int32))  19.1 us
    reduce_scatter x1, waiting for transfers between devices, per_device(): lax.psum_scatter(accumulated, 'head', scatter_dimension=1, tiled=True)  19 us
    unnamed x8, local copies, waits for them, and re-layouts  14.1 us
    add x32, other arithmetic, head_step(): return (accumulated + weights / row_total, None)  11.5 us
  transfers between devices with their start and end apart: 2, of which 2 were waited for; matrix products, arithmetic and copies ran while one was open for 1% of the time, Pallas kernels for 0%

commit v1 on v0

--- a/solution.py
+++ b/solution.py
@@ -7,6 +7,28 @@
 DH = 128
 
 
+def process_routes_all(vals, axis_no):
+    vals = jnp.moveaxis(vals, 0, axis_no)
+    vec_out = vals.shape
+    return vals.reshape(
+        *vec_out[:axis_no], vec_out[axis_no] * vec_out[axis_no + 1], *vec_out[axis_no + 2 :]
+    )
+
+
+def deliver_face(work_x, mesh_dim):
+    world_n = jax.lax.axis_size(mesh_dim)
+    arr_next = work_x[None]
+    for h in range(world_n.bit_length() - 1):
+        val = 1 << h
+        all_rows = jax.lax.ppermute(
+            arr_next, mesh_dim, [(num, num ^ val) for num in range(world_n)]
+        )
+        earlier = jnp.stack([arr_next, all_rows], axis=0)
+        mat_out = jax.lax.axis_index(mesh_dim) >> h & 1
+        arr_next = jnp.where(mat_out == 0, earlier, earlier[::-1]).reshape(-1, *work_x.shape)
+    return arr_next
+
+
 def per_device(queries, key_max, key_min, limits):
     head_count = queries.shape[1] // DH
     kv_count = key_max.shape[1] // DH
@@ -14,7 +36,11 @@
     score_scale = 1.0 / math.sqrt(DH)
     bounds = jnp.stack((key_max, key_min))
     query_rows, row_limits = (queries, limits)
-    gathered = lax.all_gather(bounds, ("row", "rep"), axis=1, tiled=True)
+
+    def remake_spots_now(my_data, xx, dim_at):
+        return process_routes_all(deliver_face(my_data, xx), dim_at)
+
+    gathered = remake_spots_now(bounds, ("row", "rep"), 1)
     page_ids = jnp.arange(gathered.shape[1], dtype=jnp.int32)
     row_count = query_rows.shape[0]
     page_count = gathered.shape[1]

time: 452 us -> 650 us (1.44)
  waiting for transfers between devices: 99.8 us -> 246 us
  local copies, waits for them, and re-layouts: 33.2 us -> 52.1 us
  other arithmetic: 24.4 us -> 40.1 us
  loops' own time: 121 us -> 132 us
    ppermute x0 -> x3, waiting for transfers between devices: none -> 225 us  [deliver_face(): jax.lax.ppermute(arr_next, mesh_dim, [(num, num ^ val) for num in range(w...]
    all_gather x1 -> x0, waiting for transfers between devices: 80.7 us -> none  [per_device(): gathered = lax.all_gather(bounds, ('row', 'rep'), axis=1, tiled=True)]
    another operation x1, loops' own time: 121 us -> 132 us  [per_device(): lax.scan(head_step, start, jnp.arange(head_count, dtype=jnp.int32))]
    reshape x0 -> x1, local copies, waits for them, and re-layouts: none -> 10.4 us  [deliver_face(): jnp.where(mat_out == 0, earlier, earlier[::-1]).reshape(-1, *work_x.shape)]
    another operation x0 -> x1, local copies, waits for them, and re-layouts: none -> 9.25 us  [per_device(): sheets = gathered.reshape(2, page_count, kv_count, DH).transpose(2, 0, 1, 3)]
    another operation x1 -> x5, other arithmetic: 1.04 us -> 10.2 us  [deliver_face(): earlier = jnp.stack([arr_next, all_rows], axis=0)]
    select_n x0 -> x2, other arithmetic: none -> 7.02 us  [deliver_face(): jnp.where(mat_out == 0, earlier, earlier[::-1]).reshape(-1, *work_x.shape)]
    unnamed x8 -> x6, local copies, waits for them, and re-layouts: 14.1 us -> 11.6 us
  transfers between devices with their start and end apart: 2 -> 4, of which waited for: 2 -> 4; matrix products, arithmetic and copies ran while one was open for 1% -> 1% of each run, Pallas kernels for 0% -> 0%
where the time goes in v1:
time: 650 us; the launch traced here: 646 us
  waiting for transfers between devices  246 us (38%)
  matrix products  156 us (24%)
  loops' own time  132 us (20%)
  local copies, waits for them, and re-layouts  52.1 us (8%)
  other arithmetic  40.1 us (6%)
  between operations  13.4 us (2%)
    ppermute x3, waiting for transfers between devices, deliver_face(): jax.lax.ppermute(arr_next, mesh_dim, [(num, num ^ val) for num in range(w...  225 us
    another operation x1, loops' own time, per_device(): lax.scan(head_step, start, jnp.arange(head_count, dtype=jnp.int32))  132 us
    dot_general x32, matrix products, head_scores(): jnp.dot(negative[head_index], sheets[kv_index, 1].T, precision=lax.Precis...  81.8 us
    dot_general x32, matrix products, head_scores(): jnp.dot(positive[head_index], sheets[kv_index, 0].T, precision=lax.Precis...  74.5 us
    reduce_scatter x1, waiting for transfers between devices, per_device(): lax.psum_scatter(accumulated, 'head', scatter_dimension=1, tiled=True)  21.5 us
    dynamic_slice x32, local copies, waits for them, and re-layouts, per_device(): lax.scan(head_step, start, jnp.arange(head_count, dtype=jnp.int32))  20.9 us
  transfers between devices with their start and end apart: 4, of which 4 were waited for; matrix products, arithmetic and copies ran while one was open for 1% of the time, Pallas kernels for 0%

profile of v1, /device:TPU:0, one launch (start us, length us, event | category | flops | bytes accessed | tf_op | source)
XLA Modules:
  0.0 646.1 jit_solution(12340322790047109485)
XLA Ops:
  12.8 2.9 collective-permute-start.1
  15.8 46.2 %collective-permute-done.1 = f32[2,2,256,512]{3,2,1,0:T(8,128)} collective-permute-done((f32[2,2,256,512]{3,2,1,0:T(8,128)}, f32[2,2,256,512]{3,2,1,0:T(8,128)}, u32[]{:S(2)}, u32[]{:S(2)}) %collective-permute-start.1) | collective-permute-done | bytes 2097184 | tf_op jit(solution)/shard_map/ppermute | solution.py:23
  64.3 2.7 reverse_select_fusion.1
  67.0 2.8 collective-permute-start.2
  73.9 176.3 %collective-permute-done.2 = f32[4,2,256,512]{3,2,1,0:T(8,128)} collective-permute-done((f32[4,2,256,512]{3,2,1,0:T(8,128)}, f32[4,2,256,512]{3,2,1,0:T(8,128)}, u32[]{:S(2)}, u32[]{:S(2)}) %collective-permute-start.2) | collective-permute-done | bytes 4194336 | tf_op jit(solution)/shard_map/ppermute | solution.py:23
  250.2 4.5 pad_maximum_fusion
  254.7 4.3 reverse_select_fusion
  259.0 10.4 %copy.11 = f32[8,2,256,512]{2,0,3,1:T(8,128)} copy(f32[8,2,256,512]{3,2,1,0:T(8,128)} %bitcast.57) | data formatting | bytes 16777216 | tf_op jit(solution)/shard_map/reshape | solution.py:28
  269.4 9.2 %reshape_reshape.3 = f32[2,2048,4,128]{1,3,2,0:T(8,128)} reshape(f32[2,8,256,512]{2,1,3,0:T(8,128)} %bitcast.58) | data formatting | bytes 16777216 | tf_op jit(solution)/shard_map/reshape;reshape | solution.py:50
  278.7 8.8 %copy.9 = f32[4,2,2048,128]{3,2,1,0:T(8,128)} copy(f32[4,2,2048,128]{2,3,0,1:T(8,128)} %bitcast.59) | data formatting | bytes 16777216
  287.4 329.4 %while.13 = (s32[]{:T(128)}, f32[128,2048]{1,0:T(8,128)S(1)}, s32[32]{0:T(128)S(1)}, f32[32,128,128]{1,2,0:T(8,128)}, f32[4,2,2048,128]{3,2,1,0:T(8,128)}, /*ind...) while((s32[]{:T(128)}, f32[128,2048]{1,0:T(8,128)S(1)}, ...), condition=%wide.region_3.4_spmd.clone, body=%wide.region_0.3_spmd.clone.sunk | while | flops 808189696 | bytes 9571708 | solution.py:70
  294.5 2.6 fusion.30
  304.8 2.6 fusion.30
  315.1 2.6 fusion.30
  325.4 2.6 fusion.30
  346.0 2.6 fusion.30
  366.5 2.6 fusion.30
  387.1 2.6 fusion.30
  407.7 2.6 fusion.30
  428.3 2.6 fusion.30
  448.9 2.6 fusion.30
  469.5 2.6 fusion.30
  490.1 2.6 fusion.30
  500.4 2.6 fusion.30
  510.7 2.6 fusion.30
  531.3 2.6 fusion.30
  551.8 2.6 fusion.30
  562.1 2.6 fusion.30
  572.4 2.6 fusion.30
  593.0 2.6 fusion.30
  613.6 2.6 fusion.30
  617.8 21.5 %reduce-scatter.2.cloned.1.call-done = f32[128,1024]{1,0:T(8,128)} async-done(((f32[128,2048]{1,0:T(8,128)}), f32[128,1024]{1,0:T(8,128)}) %reduce-scatter.2.cloned.1.call-update) | async-done | bytes 524304 | tf_op jit(solution)/shard_map/reduce_scatter | solution.py:71
  (156 shorter events, 160.3 us)
Async XLA Ops:
  6.5 632.7 %reduce-scatter.2.cloned.1.call-start = ((), (), s32[]{:S(2)}) async-start(), calls=%async_computation.1 | async-start | bytes 1572864 | tf_op jit(solution)/shard_map/reduce_scatter | solution.py:71
  8.0 2.8 collective-permute-start
  12.8 49.2 %collective-permute-start.1 = (f32[2,2,256,512]{3,2,1,0:T(8,128)}, f32[2,2,256,512]{3,2,1,0:T(8,128)}, u32[]{:S(2)}, u32[]{:S(2)}) collective-permute-start(f32[2,2,256,512]{3,2,1,0:T(8,128)} %get-tuple-element.149), channel_id=1, source_target_pairs={{0,4},{1,5},{4,0},{5,1},{8,12},{9,13},{12,8},{13,9},{2,6},{3,7},{6... | collective-permute-start | bytes 6291464 | tf_op jit(solution)/shard_map/ppermute | solution.py:23
  67.0 183.2 %collective-permute-start.2 = (f32[4,2,256,512]{3,2,1,0:T(8,128)}, f32[4,2,256,512]{3,2,1,0:T(8,128)}, u32[]{:S(2)}, u32[]{:S(2)}) collective-permute-start(f32[4,2,256,512]{3,2,1,0:T(8,128)} %bitcast.11), channel_id=1, source_target_pairs={{0,8},{1,9},{4,12},{5,13},{8,0},{9,1},{12,4},{13,5},{2,10},{3,11},... | collective-permute-start | bytes 12582920 | tf_op jit(solution)/shard_map/ppermute | solution.py:23
  278.6 8.8 %copy-start.1 = (s32[128]{0:T(128)S(1)}, s32[128]{0:T(128)}, u32[]{:S(2)}) copy-start(s32[128]{0:T(128)} %param.9) | copy-start | bytes 1540
  616.8 1.0 copy-start
Sparse Core Ops, SparseCore 0:
  617.9 21.2 reduce-scatter.1
